TPU v7x, 256 devices: a whole 4x4x8 slice. The times are simulated.
256 devices in a mesh: pair: 16 (over z, core), virt: 16 (over x, y).
Axes of the slice: x: 4, y: 4, z: 8, core: 2. Of those that a mesh axis runs over, the one named last changes fastest.
Arguments:
- amplitudes: float32 [64, 2048, 4096], P('virt', 'pair'), may hold values from -0.9 to 0.9
- integrals: float32 [64, 384, 4096], P('virt', 'pair'), may hold values from -0.09375 to 0.09375
- tile_flags: int32 [64], P('virt'), may hold values 0 or 1
- live_count: int32 [16], replicated, may hold values from 1 to 4, as said below
- pair_occ: int32 [2048, 2], P(('pair', 'virt')), may hold values from 0 to 199
- occ_energy: float32 [200], replicated, may hold values from -2.5 to -0.3
- ab_energy: float32 [384], replicated, may hold values from 0.6 to 3
Outputs:
- ladder: float32 [2048, 384], P(('pair', 'virt'))
- update: float32 [2048, 384], P(('pair', 'virt'))
Inputs may be any that keep to these rules, and one draw needn't show every extreme that they name: `live_count`: entry v is how many of the 4 slots of virt index v hold tile pairs: its slots below that number do, and the contents of the others are not to be used. At some index it is 4, and at the index half the axis away it is 1.
All inputs are finite; a program needn't handle non-finite values. No bound on the sum of `tile_flags` on one device may be relied on, other than what follows from the above.
Results may differ from a plain program's by a relative error of at most 0.0001.
Values sent between devices are 32-bit elements; how exact they have to be, the bound alone decides.
No kernel may reach another device: no remote copies, remote signals or barrier semaphores. Data moves between devices by JAX's collectives and lax.ppermute only.
A program may use at most 128 MiB of HBM per device.

v0:
```python
import jax
import jax.numpy as jnp
from jax import lax
from jax.sharding import PartitionSpec as P

TILE = 64


def swap_in_tile(rows):
    shaped = rows.reshape(rows.shape[0], TILE, TILE)
    return jnp.swapaxes(shaped, 1, 2).reshape(rows.shape)


def symmetric_amps(amp_rows, flag):
    return amp_rows + flag.astype(jnp.float32) * swap_in_tile(amp_rows)


def tile_product(amp_tile, int_rows, precision=lax.Precision.HIGH):
    return lax.dot_general(
        amp_tile,
        int_rows,
        (((1,), (1,)), ((), ())),
        precision=precision,
        preferred_element_type=jnp.float32,
    )


def on_device(amplitudes, integrals, tile_flags, live_count, pair_occ, occ_energy, ab_energy):
    slots, pair_rows, _ = amplitudes.shape
    n_virt = lax.axis_size("virt")
    half = n_virt // 2
    virt_index = lax.axis_index("virt")
    partner = (virt_index + half) % n_virt
    columns = jnp.arange(n_virt, dtype=jnp.int32)
    neighbour = columns ^ 1
    across = jnp.roll(live_count, half)
    give_one = jnp.clip((live_count - across) // 2, 0, 1)
    take_one = jnp.clip((across - live_count) // 2, 0, 1)
    keep_one = live_count - give_one
    give_two = ((keep_one == 4) & (take_one[neighbour] == 0) & (keep_one[neighbour] <= 2)).astype(
        jnp.int32
    )
    take_two = give_two[neighbour]
    keep_all = keep_one - give_two
    own_count = live_count[virt_index]
    take = take_one[virt_index]
    take_y = take_two[virt_index]
    keep = keep_all[virt_index]
    send_at = own_count - 1
    send_amp = symmetric_amps(
        lax.dynamic_index_in_dim(amplitudes, send_at, 0, keepdims=False),
        lax.dynamic_index_in_dim(tile_flags, send_at, 0, keepdims=False),
    )
    send_int = lax.dynamic_index_in_dim(integrals, send_at, 0, keepdims=False)
    perm = [(v, (v + half) % n_virt) for v in range(n_virt)]
    recv_int = lax.ppermute(send_int, "virt", perm)
    recv_amp = lax.ppermute(send_amp, "virt", perm)
    perm_y = [(v, v ^ 1) for v in range(n_virt)]
    recv_int_y = lax.ppermute(integrals[3], "virt", perm_y)
    recv_amp_y = lax.ppermute(symmetric_amps(amplitudes[3], tile_flags[3]), "virt", perm_y)

    def own_amps(slot):
        return symmetric_amps(amplitudes[slot], tile_flags[slot])

    first_two = lax.all_gather(integrals[0:2], "pair", axis=1, tiled=True)
    running = tile_product(own_amps(0), first_two[0], lax.Precision.HIGHEST)
    second = tile_product(own_amps(1), first_two[1], lax.Precision.HIGHEST)
    running = running + jnp.where(keep > 1, second, jnp.zeros_like(second))
    third_int = jnp.where(take > 0, recv_int, jnp.where(take_y > 0, recv_int_y, integrals[2]))
    third_amp = jnp.where(take > 0, recv_amp, jnp.where(take_y > 0, recv_amp_y, own_amps(2)))
    third = tile_product(third_amp, lax.all_gather(third_int, "pair", axis=0, tiled=True))
    third_live = (take > 0) | (take_y > 0) | (keep > 2)
    running = running + jnp.where(third_live, third, jnp.zeros_like(third))

    def fourth(acc):
        gathered = lax.all_gather(integrals[3], "pair", axis=0, tiled=True)
        term = tile_product(own_amps(3), gathered)
        return acc + jnp.where(keep > 3, term, jnp.zeros_like(term))

    any_full = jnp.max(keep_all) > 3
    running = lax.cond(any_full, fourth, lambda acc: acc, running)
    ab = running.shape[1]
    blocks = running.reshape(n_virt, pair_rows // n_virt, ab)
    received = lax.all_to_all(blocks, "virt", 0, 0, tiled=False)
    ladder = jnp.sum(received, axis=0)
    occ_range = jnp.arange(occ_energy.shape[0], dtype=jnp.int32)
    first_energy = jnp.sum(
        jnp.where(pair_occ[:, 0:1] == occ_range[None, :], occ_energy[None, :], 0.0), axis=1
    )
    second_energy = jnp.sum(
        jnp.where(pair_occ[:, 1:2] == occ_range[None, :], occ_energy[None, :], 0.0), axis=1
    )
    denominator = ab_energy[None, :] - first_energy[:, None] - second_energy[:, None]
    return (ladder, ladder / denominator)


def solution(mesh):
    return jax.shard_map(
        on_device,
        mesh=mesh,
        in_specs=(
            P("virt", "pair", None),
            P("virt", "pair", None),
            P("virt"),
            P(),
            P(("pair", "virt"), None),
            P(),
            P(),
        ),
        out_specs=(P(("pair", "virt"), None), P(("pair", "virt"), None)),
        check_vma=False,
    )
```

profile of v0, /device:TPU:1, one launch (start us, length us, event | category | flops | bytes accessed | tf_op | source)
XLA Modules:
  0.0 164.5 jit_solution(631864503196057487)
XLA Ops:
  7.2 0.0 copy-start.8
  7.2 0.0 copy-start.11
  7.2 0.0 all-gather.7.cloned.1.call-start
  7.2 2.2 %slice.66 = f32[2,24,4096]{2,1,0:T(8,128)} slice(f32[4,24,4096]{2,1,0:T(8,128)} %param.10), slice={[0:2], [0:24], [0:4096]} | slice | bytes 1572864 | tf_op jit(solution)/shard_map/slice | solution.py:65
  9.4 0.0 all-gather.7.cloned.1.call-update
  9.4 0.0 all-gather.9.cloned.1.call-start
  9.5 0.6 dynamic_slice.27
  11.4 0.0 copy-done.8
  11.4 0.1 slice_bitcast_fusion.8
  11.5 3.6 %collective-permute-start.2 = (f32[24,4096]{1,0:T(8,128)S(1)}, f32[24,4096]{1,0:T(8,128)S(1)}, u32[]{:S(2)}, u32[]{:S(2)}) collective-permute-start(f32[24,4096]{1,0:T(8,128)S(1)} %get-tuple-element.42), channel_id=1, source_target_pairs={{0,8},{1,9},{2,10},{3,11},{4,12},{5,13},{6,14},{7,15},{8,0},{9,1},... | collective-permute-start | bytes 1179656 | tf_op jit(solution)/shard_map/ppermute | solution.py:56
  15.1 1.3 collective-permute-start.3
  16.4 0.1 fusion.27
  16.5 0.1 fusion.23
  16.6 0.7 dynamic_slice.25
  17.2 0.7 gather_fusion
  17.9 0.7 gather_fusion.1
  18.6 0.6 fusion.24
  19.2 0.7 gather_fusion.2
  19.9 0.6 dynamic_slice.26
  21.8 1.1 collective-permute-done.2
  22.9 1.9 %collective-permute-done.3 = f32[24,4096]{1,0:T(8,128)S(1)} collective-permute-done((f32[24,4096]{1,0:T(8,128)S(1)}, f32[24,4096]{1,0:T(8,128)S(1)}, u32[]{:S(2)}, u32[]{:S(2)}) %collective-permute-start.3) | collective-permute-done | bytes 393248 | tf_op jit(solution)/shard_map/ppermute | solution.py:59
  24.8 0.8 fusion.21
  25.6 0.0 all-gather.9.cloned.1.call-update
  25.7 8.3 %fusion.25 = (f32[1,128,4096]{2,1,0:T(8,128)}, f32[1,128,4096]{2,1,0:T(8,128)}, f32[1,128,4096]{2,1,0:T(8,128)}, f32[1,128,4096]{2,1,0:T(8,128)}, f32[1,128,4096]{2,1,0:T(8,128)}) fusion(f32[4,128,4096]{2,1,0:T(8,128)} %param.9, s32[]{:T(128)S(6)} %select_n.101), kind=kLoop, calls=%fused_computation.59 | loop fusion | bytes 20971524 | tf_op jit(solution)/shard_map/slice | solution.py:63
  34.0 1.9 %copy.41 = f32[1,128,4096]{1,2,0:T(8,128)S(1)} copy(f32[1,128,4096]{2,1,0:T(8,128)} %get-tuple-element.38) | data formatting | bytes 4194304
  35.9 0.7 fusion.26
  37.2 0.1 broadcast_multiply_fusion.2
  37.4 1.2 copy.33
  38.6 1.7 %bitcast_add_fusion.3 = f32[128,4096]{0,1:T(8,128)} fusion(f32[128,64,64]{0,2,1:T(8,128)S(1)} %copy.33, f32[1,128,4096]{1,2,0:T(8,128)S(1)} %copy.41), kind=kLoop, calls=%fused_computation.17 | loop fusion | flops 524288 | bytes 6291456 | tf_op jit(solution)/shard_map/add | solution.py:15
  40.3 2.1 %collective-permute-start = (f32[128,4096]{0,1:T(8,128)}, f32[128,4096]{0,1:T(8,128)}, u32[]{:S(2)}, u32[]{:S(2)}) collective-permute-start(f32[128,4096]{0,1:T(8,128)} %bitcast_add_fusion.3), channel_id=1, source_target_pairs={{0,8},{1,9},{2,10},{3,11},{4,12},{5,13},{6,14},{7,15},{8,0},{9,1},... | collective-permute-start | bytes 6291464 | tf_op jit(solution)/shard_map/ppermute | solution.py:57
  42.4 1.9 %copy.42 = f32[1,128,4096]{1,2,0:T(8,128)S(1)} copy(f32[1,128,4096]{2,1,0:T(8,128)} %get-tuple-element.37) | data formatting | bytes 4194304
  44.9 0.1 broadcast_multiply_fusion.1
  45.1 1.2 copy.35
  46.3 1.6 bitcast_add_fusion.2
  47.8 1.2 collective-permute-start.1
  49.1 1.9 %copy.43 = f32[1,128,4096]{1,2,0:T(8,128)S(1)} copy(f32[1,128,4096]{2,1,0:T(8,128)} %get-tuple-element.36) | data formatting | bytes 4194304
  51.0 0.0 copy-start.1
  51.6 0.1 broadcast_multiply_fusion
  51.8 0.5 copy-done.1
  52.3 2.5 %copy.37 = f32[128,64,64]{0,2,1:T(8,128)} copy(f32[128,64,64]{0,1,2:T(8,128)S(1)} %bitcast.100) | data formatting | bytes 4194304 | tf_op jit(solution)/shard_map/mul | solution.py:15
  54.8 1.9 %copy.40 = f32[1,128,4096]{1,2,0:T(8,128)S(1)} copy(f32[1,128,4096]{2,1,0:T(8,128)} %get-tuple-element.39) | data formatting | bytes 4194304
  57.4 0.1 broadcast_multiply_fusion.3
  57.6 2.6 %copy.31 = f32[128,64,64]{0,2,1:T(8,128)} copy(f32[128,64,64]{0,1,2:T(8,128)S(1)} %bitcast.101) | data formatting | bytes 4194304 | tf_op jit(solution)/shard_map/mul | solution.py:15
  60.1 0.6 dynamic_slice.24
  60.7 2.9 %copy.39 = f32[1,128,4096]{1,2,0:T(8,128)} copy(f32[1,128,4096]{2,1,0:T(8,128)} %get-tuple-element.40) | data formatting | bytes 4194304
  64.2 1.8 %broadcast_multiply_fusion.4 = f32[1,128,4096]{1,2,0:T(8,128)S(1)} fusion(f32[1,128,4096]{1,2,0:T(8,128)} %copy.39, f32[]{:T(128)} %bitcast.7), kind=kLoop, calls=%fused_computation.30 | loop fusion | flops 524288 | bytes 4194308 | tf_op jit(solution)/shard_map/mul | solution.py:15
  66.0 2.5 %copy.29 = f32[128,64,64]{0,2,1:T(8,128)} copy(f32[128,64,64]{0,1,2:T(8,128)S(1)} %bitcast.102) | data formatting | bytes 4194304 | tf_op jit(solution)/shard_map/mul | solution.py:15
  70.5 0.0 copy-start
  70.5 0.0 copy-start.3
  70.5 3.4 %bitcast_add_fusion.4 = f32[1,128,4096]{1,2,0:T(8,128)} fusion(f32[1,128,4096]{1,2,0:T(8,128)S(1)} %copy.40, f32[128,64,64]{0,2,1:T(8,128)} %copy.31), kind=kLoop, calls=%fused_computation.19 | loop fusion | flops 524288 | bytes 6291456 | tf_op jit(solution)/shard_map/add | solution.py:15
  74.0 1.6 bitcast_add_fusion.5
  75.5 11.9 %collective-permute-done = f32[128,4096]{0,1:T(8,128)} collective-permute-done((f32[128,4096]{0,1:T(8,128)}, f32[128,4096]{0,1:T(8,128)}, u32[]{:S(2)}, u32[]{:S(2)}) %collective-permute-start) | collective-permute-done | bytes 2097184 | tf_op jit(solution)/shard_map/ppermute | solution.py:57
  87.4 6.4 %collective-permute-done.1 = f32[128,4096]{0,1:T(8,128)} collective-permute-done((f32[128,4096]{0,1:T(8,128)}, f32[128,4096]{0,1:T(8,128)}, u32[]{:S(2)}, u32[]{:S(2)}) %collective-permute-start.1) | collective-permute-done | bytes 2097184 | tf_op jit(solution)/shard_map/ppermute | solution.py:60
  93.8 2.3 %fusion.11 = f32[128,4096]{0,1:T(8,128)} fusion(f32[128,4096]{0,1:T(8,128)} %collective-permute-done, f32[128,4096]{0,1:T(8,128)} %collective-permute-done.1, f32[128,64,64]{0,2,1:T(8,128)S(1)} %copy-done.7, f32[1,128,4096]{1,2,0:T(8,128)S(1)} %copy-done.2, pred[]{:T(512)} %bitcast.21, pred[]{:T(512)} %bitcast.20), kind=kLoop, calls=%fused_computation.15 | loop fusion | flops 1572864 | bytes 10485762 | tf_op jit(solution)/shard_map/jit(_where)/select_n | solution.py:70
  96.1 9.5 %fusion.17 = f32[128,384]{1,0:T(8,128)S(1)} fusion(f32[2,384,4096]{2,1,0:T(8,128)} %all-gather.7.cloned.1.call-done, f32[1,128,4096]{1,2,0:T(8,128)S(1)} %copy-done.4, pred[]{:T(512)S(6)} %gt.29), kind=kOutput, calls=%fused_computation.23 | convolution fusion | flops 2415968256 | bytes 8585217 | tf_op jit(solution)/shard_map/dot_general | solution.py:19
  105.7 0.0 copy-done.5
  105.7 9.8 %fusion.14 = f32[128,384]{1,0:T(8,128)S(1)} fusion(f32[128,384]{1,0:T(8,128)S(1)} %fusion.17, f32[2,384,4096]{2,1,0:T(8,128)} %all-gather.7.cloned.1.call-done, f32[1,128,4096]{1,2,0:T(8,128)S(1)} %copy-done.5), kind=kOutput, calls=%fused_computation.22 | convolution fusion | flops 2415968256 | bytes 8781824 | tf_op jit(solution)/shard_map/dot_general | solution.py:19
  115.5 20.6 %all-gather.9.cloned.1.call-done = f32[384,4096]{1,0:T(8,128)} async-done(((f32[24,4096]{1,0:T(8,128)}), f32[384,4096]{1,0:T(8,128)}) %all-gather.9.cloned.1.call-update) | async-done | bytes 6291472 | tf_op jit(solution)/shard_map/all_gather | solution.py:71
  136.1 7.1 %fusion.20 = f32[128,384]{1,0:T(8,128)} fusion(f32[128,384]{1,0:T(8,128)S(1)} %fusion.14, f32[128,4096]{0,1:T(8,128)S(1)} %copy-done.6, f32[384,4096]{1,0:T(8,128)} %all-gather.9.cloned.1.call-done, pred[]{:T(512)S(6)} %or.7), kind=kOutput, calls=%fused_computation.25 | convolution fusion | flops 1208057856 | bytes 8781825 | tf_op jit(solution)/shard_map/dot_general | solution.py:19
  143.2 6.7 %all-to-all-start = ((f32[16,8,384]{2,1,0:T(8,128)}), f32[16,8,384]{2,1,0:T(8,128)S(1)}, u32[]{:S(2)}, u32[]{:S(2)}) async-start(f32[16,8,384]{2,1,0:T(8,128)} %bitcast.42), calls=%async_computation | async-start | bytes 393216 | tf_op jit(solution)/shard_map/all_to_all | solution.py:84
  149.9 0.2 select_reduce_fusion.1
  150.1 6.8 %all-to-all-done = f32[16,8,384]{2,1,0:T(8,128)S(1)} async-done(((f32[16,8,384]{2,1,0:T(8,128)}), f32[16,8,384]{2,1,0:T(8,128)S(1)}, u32[]{:S(2)}, u32[]{:S(2)}) %all-to-all-start) | async-done | bytes 196640 | tf_op jit(solution)/shard_map/all_to_all | solution.py:84
  156.9 0.0 copy-start.9
  156.9 0.7 subtract_divide_fusion
  (27 shorter events, 0.1 us)
Async XLA Ops:
  7.2 4.2 %copy-start.8 = (f32[4,24,4096]{2,1,0:T(8,128)S(1)}, f32[4,24,4096]{2,1,0:T(8,128)}, u32[]{:S(2)}) copy-start(f32[4,24,4096]{2,1,0:T(8,128)} %param.10) | copy-start | bytes 4718596
  7.2 2.3 %copy-start.11 = (s32[16]{0:T(128)S(1)}, s32[16]{0:T(128)}, u32[]{:S(2)}) copy-start(s32[16]{0:T(128)} %param.12) | copy-start | bytes 196
  7.2 88.9 %all-gather.7.cloned.1.call-start = ((), (), s32[]{:S(2)}) async-start(), calls=%async_computation.2 | async-start | bytes 13369344 | tf_op jit(solution)/shard_map/all_gather | solution.py:65
  9.4 126.7 %all-gather.9.cloned.1.call-start = ((), (), s32[]{:S(2)}) async-start(), calls=%async_computation.3 | async-start | bytes 6684672 | tf_op jit(solution)/shard_map/all_gather | solution.py:71
  11.5 11.4 %collective-permute-start.2 = (f32[24,4096]{1,0:T(8,128)S(1)}, f32[24,4096]{1,0:T(8,128)S(1)}, u32[]{:S(2)}, u32[]{:S(2)}) collective-permute-start(f32[24,4096]{1,0:T(8,128)S(1)} %get-tuple-element.42), channel_id=1, source_target_pairs={{0,8},{1,9},{2,10},{3,11},{4,12},{5,13},{6,14},{7,15},{8,0},{9,1},... | collective-permute-start | bytes 1179656 | tf_op jit(solution)/shard_map/ppermute | solution.py:56
  15.1 9.7 %collective-permute-start.3 = (f32[24,4096]{1,0:T(8,128)S(1)}, f32[24,4096]{1,0:T(8,128)S(1)}, u32[]{:S(2)}, u32[]{:S(2)}) collective-permute-start(f32[24,4096]{1,0:T(8,128)S(1)} %get-tuple-element.41), channel_id=1, source_target_pairs={{0,1},{1,0},{2,3},{3,2},{4,5},{5,4},{6,7},{7,6},{8,9},{9,8},{10,11... | collective-permute-start | bytes 1179656 | tf_op jit(solution)/shard_map/ppermute | solution.py:59
  34.0 1.9 %copy-start.10 = (s32[4]{0:T(128)S(1)}, s32[4]{0:T(128)}, u32[]{:S(2)}) copy-start(s32[4]{0:T(128)} %param.11) | copy-start | bytes 52
  40.3 47.1 %collective-permute-start = (f32[128,4096]{0,1:T(8,128)}, f32[128,4096]{0,1:T(8,128)}, u32[]{:S(2)}, u32[]{:S(2)}) collective-permute-start(f32[128,4096]{0,1:T(8,128)} %bitcast_add_fusion.3), channel_id=1, source_target_pairs={{0,8},{1,9},{2,10},{3,11},{4,12},{5,13},{6,14},{7,15},{8,0},{9,1},... | collective-permute-start | bytes 6291464 | tf_op jit(solution)/shard_map/ppermute | solution.py:57
  47.8 46.0 %collective-permute-start.1 = (f32[128,4096]{0,1:T(8,128)}, f32[128,4096]{0,1:T(8,128)}, u32[]{:S(2)}, u32[]{:S(2)}) collective-permute-start(f32[128,4096]{0,1:T(8,128)} %bitcast_add_fusion.2), channel_id=1, source_target_pairs={{0,1},{1,0},{2,3},{3,2},{4,5},{5,4},{6,7},{7,6},{8,9},{9,8},{10,11... | collective-permute-start | bytes 6291464 | tf_op jit(solution)/shard_map/ppermute | solution.py:60
  51.0 1.3 copy-start.1
  70.5 3.5 %copy-start = (f32[1,128,4096]{1,2,0:T(8,128)S(1)}, f32[1,128,4096]{1,2,0:T(8,128)}, u32[]{:S(2)}) copy-start(f32[1,128,4096]{1,2,0:T(8,128)} %copy.39) | copy-start | bytes 6291460
  70.5 3.5 %copy-start.3 = (f32[128,64,64]{0,2,1:T(8,128)S(1)}, f32[128,64,64]{0,2,1:T(8,128)}, u32[]{:S(2)}) copy-start(f32[128,64,64]{0,2,1:T(8,128)} %copy.29) | copy-start | bytes 6291460
  74.0 19.9 %copy-start.2 = (f32[1,128,4096]{1,2,0:T(8,128)S(1)}, f32[1,128,4096]{1,2,0:T(8,128)}, u32[]{:S(2)}) copy-start(f32[1,128,4096]{1,2,0:T(8,128)} %copy-done.1) | copy-start | bytes 6291460
  74.0 19.9 %copy-start.7 = (f32[128,64,64]{0,2,1:T(8,128)S(1)}, f32[128,64,64]{0,2,1:T(8,128)}, u32[]{:S(2)}) copy-start(f32[128,64,64]{0,2,1:T(8,128)} %copy.37) | copy-start | bytes 6291460
  75.5 20.6 %copy-start.4 = (f32[1,128,4096]{1,2,0:T(8,128)S(1)}, f32[1,128,4096]{1,2,0:T(8,128)}, u32[]{:S(2)}) copy-start(f32[1,128,4096]{1,2,0:T(8,128)} %bitcast_add_fusion.4) | copy-start | bytes 6291460
  96.1 9.5 %copy-start.5 = (f32[1,128,4096]{1,2,0:T(8,128)S(1)}, f32[1,128,4096]{1,2,0:T(8,128)}, u32[]{:S(2)}) copy-start(f32[1,128,4096]{1,2,0:T(8,128)} %bitcast_add_fusion.5) | copy-start | bytes 6291460
  105.7 30.4 %copy-start.6 = (f32[128,4096]{0,1:T(8,128)S(1)}, f32[128,4096]{0,1:T(8,128)}, u32[]{:S(2)}) copy-start(f32[128,4096]{0,1:T(8,128)} %fusion.11) | copy-start | bytes 6291460
  143.2 6.7 %copy-start.14 = (s32[8,2]{0,1:T(2,128)S(1)}, s32[8,2]{0,1:T(2,128)}, u32[]{:S(2)}) copy-start(s32[8,2]{0,1:T(2,128)} %param.13) | copy-start | bytes 196
  143.2 6.7 %copy-start.13 = (f32[200]{0:T(256)S(1)}, f32[200]{0:T(256)}, u32[]{:S(2)}) copy-start(f32[200]{0:T(256)} %param.14) | copy-start | bytes 2404
  143.2 13.7 %copy-start.12 = (f32[384]{0:T(512)S(1)}, f32[384]{0:T(512)}, u32[]{:S(2)}) copy-start(f32[384]{0:T(512)} %param.15) | copy-start | bytes 4612
  143.2 13.7 %all-to-all-start = ((f32[16,8,384]{2,1,0:T(8,128)}), f32[16,8,384]{2,1,0:T(8,128)S(1)}, u32[]{:S(2)}, u32[]{:S(2)}) async-start(f32[16,8,384]{2,1,0:T(8,128)} %bitcast.42), calls=%async_computation | async-start | bytes 393216 | tf_op jit(solution)/shard_map/all_to_all | solution.py:84
  156.9 0.7 copy-start.9
Sparse Core Ops, SparseCore 0:
  9.8 79.7 all-gather.6
  91.5 44.5 all-gather.8
where the time goes:
time: 165 us; the launch traced here: 164 us
  waiting for transfers between devices  48.7 us (30%)
  local copies, waits for them, and re-layouts  36.9 us (22%)
  matrix products  26.5 us (16%)
  between operations  22 us (13%)
  other arithmetic  15.4 us (9%)
  starting transfers between devices  15 us (9%)
    dot_general x3, matrix products, tile_product(): lax.dot_general(amp_tile, int_rows, (((1,), (1,)), ((), ())), precision=p...  26.5 us
    all_gather x1, waiting for transfers between devices, on_device(): lax.all_gather(third_int, 'pair', axis=0, tiled=True)  20.6 us
    ppermute x1, waiting for transfers between devices, on_device(): recv_amp = lax.ppermute(send_amp, 'virt', perm)  11.9 us
    unnamed x35, local copies, waits for them, and re-layouts  11.2 us
    mul x5, local copies, waits for them, and re-layouts, symmetric_amps(): return amp_rows + flag.astype(jnp.float32) * swap_in_tile(amp_rows)  10 us
    slice x2, local copies, waits for them, and re-layouts, own_amps(): return symmetric_amps(amplitudes[slot], tile_flags[slot])  8.97 us
    add x4, other arithmetic, symmetric_amps(): return amp_rows + flag.astype(jnp.float32) * swap_in_tile(amp_rows)  8.24 us
    all_to_all x1, waiting for transfers between devices, on_device(): received = lax.all_to_all(blocks, 'virt', 0, 0, tiled=False)  6.75 us
  transfers between devices with their start and end apart: 7, of which 6 were waited for; matrix products, arithmetic and copies ran while one was open for 41% of the time, Pallas kernels for 0%

commit v1 on v0

--- a/solution.py
+++ b/solution.py
@@ -4,6 +4,19 @@
 from jax.sharding import PartitionSpec as P
 
 TILE = 64
+
+
+def ring_gather(value, axis, dim):
+    ways = lax.axis_size(axis)
+    up = [(d, (d + 1) % ways) for d in range(ways)]
+    down = [(d, (d - 1) % ways) for d in range(ways)]
+    earlier, later = ([value], [value])
+    for _ in range(ways // 2):
+        earlier.append(lax.ppermute(earlier[-1], axis, up))
+    for _ in range((ways - 1) // 2):
+        later.append(lax.ppermute(later[-1], axis, down))
+    line = jnp.concatenate([*earlier[::-1], *later[1:]], axis=dim)
+    return jnp.roll(line, (lax.axis_index(axis) - ways // 2) * value.shape[dim], axis=dim)
 
 
 def swap_in_tile(rows):
@@ -68,7 +81,7 @@
     running = running + jnp.where(keep > 1, second, jnp.zeros_like(second))
     third_int = jnp.where(take > 0, recv_int, jnp.where(take_y > 0, recv_int_y, integrals[2]))
     third_amp = jnp.where(take > 0, recv_amp, jnp.where(take_y > 0, recv_amp_y, own_amps(2)))
-    third = tile_product(third_amp, lax.all_gather(third_int, "pair", axis=0, tiled=True))
+    third = tile_product(third_amp, ring_gather(third_int, "pair", 0))
     third_live = (take > 0) | (take_y > 0) | (keep > 2)
     running = running + jnp.where(third_live, third, jnp.zeros_like(third))
 

time: 165 us -> 253 us (1.53); the launches traced: 164 us -> 249 us
  local copies, waits for them, and re-layouts: 36.9 us -> 79.7 us
  starting transfers between devices: 15 us -> 42.2 us
  waiting for transfers between devices: 48.7 us -> 64.4 us
    unnamed x35 -> x56, local copies, waits for them, and re-layouts: 11.2 us -> 53.8 us
    ppermute x1, waiting for transfers between devices: 1.1 us -> 43.3 us  [on_device(): recv_int = lax.ppermute(send_int, 'virt', perm)]
    ppermute x0 -> x15, starting transfers between devices: none -> 28.4 us  [the longest x7 21.6 us: ring_gather(): later.append(lax.ppermute(later[-1], axis, down))]
    all_gather x1 -> x0, waiting for transfers between devices: 20.6 us -> none  [on_device(): lax.all_gather(third_int, 'pair', axis=0, tiled=True)]
    ppermute x0 -> x15, waiting for transfers between devices: none -> 14.5 us  [the longest x7 11.1 us: ring_gather(): later.append(lax.ppermute(later[-1], axis, down))]
    ppermute x1, waiting for transfers between devices: 11.9 us -> 0.01 us  [on_device(): recv_amp = lax.ppermute(send_amp, 'virt', perm)]
    ppermute x1, waiting for transfers between devices: 6.41 us -> 0.01 us  [on_device(): lax.ppermute(symmetric_amps(amplitudes[3], tile_flags[3]), 'virt', perm_y)]
    ppermute x1, starting transfers between devices: 3.65 us -> 0.09 us  [on_device(): recv_int = lax.ppermute(send_int, 'virt', perm)]
  transfers between devices with their start and end apart: 7 -> 21, of which waited for: 6 -> 7; matrix products, arithmetic and copies ran while one was open for 41% -> 37% of each run, Pallas kernels for 0% -> 0%
where the time goes in v1:
time: 253 us; the launch traced here: 249 us
  local copies, waits for them, and re-layouts  79.7 us (32%)
  waiting for transfers between devices  64.4 us (25%)
  starting transfers between devices  42.2 us (17%)
  matrix products  26.4 us (10%)
  between operations  22.2 us (9%)
  other arithmetic  14.6 us (6%)
    unnamed x56, local copies, waits for them, and re-layouts  53.8 us
    ppermute x1, waiting for transfers between devices, on_device(): recv_int = lax.ppermute(send_int, 'virt', perm)  43.3 us
    dot_general x3, matrix products, tile_product(): lax.dot_general(amp_tile, int_rows, (((1,), (1,)), ((), ())), precision=p...  26.4 us
    ppermute x7, starting transfers between devices, ring_gather(): later.append(lax.ppermute(later[-1], axis, down))  21.6 us
    ppermute x7, waiting for transfers between devices, ring_gather(): later.append(lax.ppermute(later[-1], axis, down))  11.1 us
    mul x5, local copies, waits for them, and re-layouts, symmetric_amps(): return amp_rows + flag.astype(jnp.float32) * swap_in_tile(amp_rows)  8.98 us
    slice x2, local copies, waits for them, and re-layouts, own_amps(): return symmetric_amps(amplitudes[slot], tile_flags[slot])  8.77 us
    all_to_all x1, starting transfers between devices, on_device(): received = lax.all_to_all(blocks, 'virt', 0, 0, tiled=False)  7.24 us
  transfers between devices with their start and end apart: 21, of which 7 were waited for; matrix products, arithmetic and copies ran while one was open for 37% of the time, Pallas kernels for 0%

profile of v1, /device:TPU:1, one launch (start us, length us, event | category | flops | bytes accessed | tf_op | source)
XLA Modules:
  0.0 249.4 jit_solution(3620531803509570958)
XLA Ops:
  7.2 2.1 slice.66
  9.3 1.2 dynamic_slice.31
  11.9 8.1 %fusion.33 = (f32[1,128,4096]{2,1,0:T(8,128)}, f32[1,128,4096]{2,1,0:T(8,128)}, f32[1,128,4096]{2,1,0:T(8,128)}, f32[1,128,4096]{2,1,0:T(8,128)}, f32[1,128,4096]{2,1,0:T(8,128)}) fusion(f32[4,128,4096]{2,1,0:T(8,128)} %param.9, s32[]{:T(128)S(6)} %select_n.114), kind=kLoop, calls=%fused_computation.94 | loop fusion | bytes 20971524 | tf_op jit(solution)/shard_map/slice | solution.py:76
  20.6 1.9 copy.41
  23.5 1.2 copy.33
  24.8 1.6 bitcast_add_fusion.3
  26.4 3.6 %collective-permute-start = (f32[128,4096]{0,1:T(8,128)}, f32[128,4096]{0,1:T(8,128)}, u32[]{:S(2)}, u32[]{:S(2)}) collective-permute-start(f32[128,4096]{0,1:T(8,128)} %bitcast_add_fusion.3), channel_id=1, source_target_pairs={{0,8},{1,9},{2,10},{3,11},{4,12},{5,13},{6,14},{7,15},{8,0},{9,1},... | collective-permute-start | bytes 6291464 | tf_op jit(solution)/shard_map/ppermute | solution.py:70
  30.1 1.5 collective-permute-start.3
  33.7 1.9 copy.42
  39.6 43.3 %collective-permute-done.2 = f32[24,4096]{1,0:T(8,128)S(1)} collective-permute-done((f32[24,4096]{1,0:T(8,128)S(1)}, f32[24,4096]{1,0:T(8,128)S(1)}, u32[]{:S(2)}, u32[]{:S(2)}) %collective-permute-start.2) | collective-permute-done | bytes 393248 | tf_op jit(solution)/shard_map/ppermute | solution.py:69
  82.9 1.1 fusion.28
  84.0 4.0 %collective-permute-start.4 = (f32[24,4096]{1,0:T(8,128)S(1)}, f32[24,4096]{1,0:T(8,128)S(1)}, u32[]{:S(2)}, u32[]{:S(2)}) collective-permute-start(f32[24,4096]{1,0:T(8,128)S(1)} %fusion.28), channel_id=1, source_target_pairs={{0,16},{16,32},{32,48},{48,64},{64,80},{80,96},{96,112},{112,128},... | collective-permute-start | bytes 1179656 | tf_op jit(solution)/shard_map/ppermute | solution.py:15
  88.1 1.2 copy.35
  89.4 3.4 %collective-permute-done.4 = f32[24,4096]{1,0:T(8,128)S(1)} collective-permute-done((f32[24,4096]{1,0:T(8,128)S(1)}, f32[24,4096]{1,0:T(8,128)S(1)}, u32[]{:S(2)}, u32[]{:S(2)}) %collective-permute-start.4) | collective-permute-done | bytes 393248 | tf_op jit(solution)/shard_map/ppermute | solution.py:15
  92.7 2.5 collective-permute-start.5
  95.2 1.7 bitcast_add_fusion.2
  96.9 1.3 collective-permute-start.1
  98.1 1.9 copy.40
  100.7 1.4 collective-permute-start.12
  102.6 1.2 copy.31
  103.8 4.5 %collective-permute-done.12 = f32[24,4096]{1,0:T(8,128)} collective-permute-done((f32[24,4096]{1,0:T(8,128)S(1)}, f32[24,4096]{1,0:T(8,128)}, u32[]{:S(2)}, u32[]{:S(2)}) %collective-permute-start.12) | collective-permute-done | bytes 393248 | tf_op jit(solution)/shard_map/ppermute | solution.py:17
  108.3 1.8 collective-permute-start.13
  110.1 1.6 bitcast_add_fusion.4
  111.7 1.9 copy.39
  114.2 1.9 collective-permute-done.13
  116.1 2.8 %collective-permute-start.14 = (f32[24,4096]{1,0:T(8,128)}, f32[24,4096]{1,0:T(8,128)}, u32[]{:S(2)}, u32[]{:S(2)}) collective-permute-start(f32[24,4096]{1,0:T(8,128)} %collective-permute-done.13), channel_id=1, source_target_pairs={{0,240},{16,0},{32,16},{48,32},{64,48},{80,64},{96,80},{112,96},{1... | collective-permute-start | bytes 1179656 | tf_op jit(solution)/shard_map/ppermute | solution.py:17
  119.0 1.2 copy.29
  120.3 3.7 %collective-permute-done.14 = f32[24,4096]{1,0:T(8,128)} collective-permute-done((f32[24,4096]{1,0:T(8,128)}, f32[24,4096]{1,0:T(8,128)}, u32[]{:S(2)}, u32[]{:S(2)}) %collective-permute-start.14) | collective-permute-done | bytes 393248 | tf_op jit(solution)/shard_map/ppermute | solution.py:17
  123.9 3.7 %collective-permute-start.15 = (f32[24,4096]{1,0:T(8,128)}, f32[24,4096]{1,0:T(8,128)}, u32[]{:S(2)}, u32[]{:S(2)}) collective-permute-start(f32[24,4096]{1,0:T(8,128)} %collective-permute-done.14), channel_id=1, source_target_pairs={{0,240},{16,0},{32,16},{48,32},{64,48},{80,64},{96,80},{112,96},{1... | collective-permute-start | bytes 1179656 | tf_op jit(solution)/shard_map/ppermute | solution.py:17
  127.6 1.6 bitcast_add_fusion.5
  129.3 1.9 copy.43
  131.8 4.5 %collective-permute-start.16 = (f32[24,4096]{1,0:T(8,128)}, f32[24,4096]{1,0:T(8,128)}, u32[]{:S(2)}, u32[]{:S(2)}) collective-permute-start(f32[24,4096]{1,0:T(8,128)} %collective-permute-done.15), channel_id=1, source_target_pairs={{0,240},{16,0},{32,16},{48,32},{64,48},{80,64},{96,80},{112,96},{1... | collective-permute-start | bytes 1179656 | tf_op jit(solution)/shard_map/ppermute | solution.py:17
  136.4 1.5 broadcast_multiply_fusion
  139.1 4.1 %copy.37 = f32[128,64,64]{0,2,1:T(8,128)} copy(f32[128,64,64]{0,1,2:T(8,128)} %bitcast.97) | data formatting | bytes 4194304 | tf_op jit(solution)/shard_map/mul | solution.py:28
  144.5 3.1 %collective-permute-start.17 = (f32[24,4096]{1,0:T(8,128)}, f32[24,4096]{1,0:T(8,128)S(1)}, u32[]{:S(2)}, u32[]{:S(2)}) collective-permute-start(f32[24,4096]{1,0:T(8,128)} %collective-permute-done.16), channel_id=1, source_target_pairs={{0,240},{16,0},{32,16},{48,32},{64,48},{80,64},{96,80},{112,96},{1... | collective-permute-start | bytes 1179656 | tf_op jit(solution)/shard_map/ppermute | solution.py:17
  147.6 3.3 %fusion.13 = f32[128,4096]{0,1:T(8,128)} fusion(f32[128,4096]{0,1:T(8,128)} %collective-permute-done, f32[128,4096]{0,1:T(8,128)} %collective-permute-done.1, f32[128,64,64]{0,2,1:T(8,128)} %copy.37, f32[1,128,4096]{1,2,0:T(8,128)S(1)} %copy.43, pred[]{:T(512)} %bitcast.21, pred[]{:T(512)} %bitcast.20), kind=kLoop, calls=%fused_computation.17 | loop fusion | flops 1572864 | bytes 10485762 | tf_op jit(solution)/shard_map/jit(_where)/select_n | solution.py:83
  150.9 1.0 collective-permute-done.17
  151.9 4.3 %collective-permute-start.18 = (f32[24,4096]{1,0:T(8,128)S(1)}, f32[24,4096]{1,0:T(8,128)S(1)}, u32[]{:S(2)}, u32[]{:S(2)}) collective-permute-start(f32[24,4096]{1,0:T(8,128)S(1)} %collective-permute-done.17), channel_id=1, source_target_pairs={{0,240},{16,0},{32,16},{48,32},{64,48},{80,64},{96,80},{112,96},{1... | collective-permute-start | bytes 1179656 | tf_op jit(solution)/shard_map/ppermute | solution.py:17
  157.0 1.8 constant_dynamic-update-slice_fusion.30
  158.8 1.8 constant_dynamic-update-slice_fusion.29
  160.5 1.8 constant_dynamic-update-slice_fusion.28
  162.3 1.8 constant_dynamic-update-slice_fusion.27
  164.1 1.8 constant_dynamic-update-slice_fusion.26
  168.2 1.8 constant_dynamic-update-slice_fusion.22
  170.0 1.8 constant_dynamic-update-slice_fusion.21
  171.7 1.9 constant_dynamic-update-slice_fusion.20
  173.6 1.8 constant_dynamic-update-slice_fusion.19
  175.4 1.8 constant_dynamic-update-slice_fusion.18
  179.5 1.8 constant_dynamic-update-slice_fusion.14
  181.3 1.8 constant_dynamic-update-slice_fusion.13
  183.1 1.8 constant_dynamic-update-slice_fusion.12
  184.8 1.8 constant_dynamic-update-slice_fusion.11
  186.6 1.8 constant_dynamic-update-slice_fusion.10
  190.7 1.8 constant_dynamic-update-slice_fusion.6
  192.5 1.8 constant_dynamic-update-slice_fusion.5
  194.3 1.8 constant_dynamic-update-slice_fusion.4
  196.1 1.8 constant_dynamic-update-slice_fusion.3
  197.9 1.8 constant_dynamic-update-slice_fusion.2
  199.6 0.8 constant_dynamic-update-slice_fusion.1
  201.2 9.5 %fusion.19 = f32[128,384]{1,0:T(8,128)S(1)} fusion(f32[2,384,4096]{2,1,0:T(8,128)} %all-gather.6.cloned.1.call-done, f32[1,128,4096]{1,2,0:T(8,128)S(1)} %copy-done, pred[]{:T(512)S(6)} %gt.29), kind=kOutput, calls=%fused_computation.25 | convolution fusion | flops 2415968256 | bytes 8585217 | tf_op jit(solution)/shard_map/dot_general | solution.py:32
  210.8 9.6 %fusion.16 = f32[128,384]{1,0:T(8,128)S(1)} fusion(f32[128,384]{1,0:T(8,128)S(1)} %fusion.19, f32[2,384,4096]{2,1,0:T(8,128)} %all-gather.6.cloned.1.call-done, f32[1,128,4096]{1,2,0:T(8,128)S(1)} %copy-done.1), kind=kOutput, calls=%fused_computation.24 | convolution fusion | flops 2415968256 | bytes 8781824 | tf_op jit(solution)/shard_map/dot_general | solution.py:32
  220.4 7.2 %fusion.25 = f32[128,384]{1,0:T(8,128)} fusion(f32[128,384]{1,0:T(8,128)S(1)} %fusion.16, f32[128,4096]{0,1:T(8,128)S(1)} %copy-done.2, f32[768,4096]{1,0:T(8,128)} %constant_dynamic-update-slice_fusion, s32[]{:T(128)S(6)} %select_n.123, pred[]{:T(512)S(6)} %or.7), kind=kOutput, calls=%fused_computation.27 | convolution fusion | flops 1208057856 | bytes 8781829 | tf_op jit(solution)/shard_map/dot_general | solution.py:32
  227.6 7.2 %all-to-all-start = ((f32[16,8,384]{2,1,0:T(8,128)}), f32[16,8,384]{2,1,0:T(8,128)S(1)}, u32[]{:S(2)}, u32[]{:S(2)}) async-start(f32[16,8,384]{2,1,0:T(8,128)} %bitcast.42), calls=%async_computation | async-start | bytes 393216 | tf_op jit(solution)/shard_map/all_to_all | solution.py:97
  235.1 6.7 %all-to-all-done = f32[16,8,384]{2,1,0:T(8,128)S(1)} async-done(((f32[16,8,384]{2,1,0:T(8,128)}), f32[16,8,384]{2,1,0:T(8,128)S(1)}, u32[]{:S(2)}, u32[]{:S(2)}) %all-to-all-start) | async-done | bytes 196640 | tf_op jit(solution)/shard_map/all_to_all | solution.py:97
  (76 shorter events, 16.1 us)
Async XLA Ops:
  7.2 194.1 %all-gather.6.cloned.1.call-start = ((), (), s32[]{:S(2)}) async-start(), calls=%async_computation.2 | async-start | bytes 13369344 | tf_op jit(solution)/shard_map/all_gather | solution.py:78
  11.9 8.1 %copy-start.5 = (s32[4]{0:T(128)S(1)}, s32[4]{0:T(128)}, u32[]{:S(2)}) copy-start(s32[4]{0:T(128)} %param.11) | copy-start | bytes 52
  22.6 7.4 %copy-start.3 = (f32[4,24,4096]{2,1,0:T(8,128)S(1)}, f32[4,24,4096]{2,1,0:T(8,128)}, u32[]{:S(2)}) copy-start(f32[4,24,4096]{2,1,0:T(8,128)} %param.10) | copy-start | bytes 4718596
  22.6 9.0 %copy-start.6 = (s32[16]{0:T(128)S(1)}, s32[16]{0:T(128)}, u32[]{:S(2)}) copy-start(s32[16]{0:T(128)} %param.12) | copy-start | bytes 196
  26.4 121.3 %collective-permute-start = (f32[128,4096]{0,1:T(8,128)}, f32[128,4096]{0,1:T(8,128)}, u32[]{:S(2)}, u32[]{:S(2)}) collective-permute-start(f32[128,4096]{0,1:T(8,128)} %bitcast_add_fusion.3), channel_id=1, source_target_pairs={{0,8},{1,9},{2,10},{3,11},{4,12},{5,13},{6,14},{7,15},{8,0},{9,1},... | collective-permute-start | bytes 6291464 | tf_op jit(solution)/shard_map/ppermute | solution.py:70
  30.0 52.9 %collective-permute-start.2 = (f32[24,4096]{1,0:T(8,128)S(1)}, f32[24,4096]{1,0:T(8,128)S(1)}, u32[]{:S(2)}, u32[]{:S(2)}) collective-permute-start(f32[24,4096]{1,0:T(8,128)S(1)} %get-tuple-element.42), channel_id=1, source_target_pairs={{0,8},{1,9},{2,10},{3,11},{4,12},{5,13},{6,14},{7,15},{8,0},{9,1},... | collective-permute-start | bytes 1179656 | tf_op jit(solution)/shard_map/ppermute | solution.py:69
  30.1 52.8 %collective-permute-start.3 = (f32[24,4096]{1,0:T(8,128)S(1)}, f32[24,4096]{1,0:T(8,128)}, u32[]{:S(2)}, u32[]{:S(2)}) collective-permute-start(f32[24,4096]{1,0:T(8,128)S(1)} %get-tuple-element.41), channel_id=1, source_target_pairs={{0,1},{1,0},{2,3},{3,2},{4,5},{5,4},{6,7},{7,6},{8,9},{9,8},{10,11... | collective-permute-start | bytes 1179656 | tf_op jit(solution)/shard_map/ppermute | solution.py:72
  84.0 8.7 %collective-permute-start.4 = (f32[24,4096]{1,0:T(8,128)S(1)}, f32[24,4096]{1,0:T(8,128)S(1)}, u32[]{:S(2)}, u32[]{:S(2)}) collective-permute-start(f32[24,4096]{1,0:T(8,128)S(1)} %fusion.28), channel_id=1, source_target_pairs={{0,16},{16,32},{32,48},{48,64},{64,80},{80,96},{96,112},{112,128},... | collective-permute-start | bytes 1179656 | tf_op jit(solution)/shard_map/ppermute | solution.py:15
  92.7 9.4 %collective-permute-start.5 = (f32[24,4096]{1,0:T(8,128)S(1)}, f32[24,4096]{1,0:T(8,128)S(1)}, u32[]{:S(2)}, u32[]{:S(2)}) collective-permute-start(f32[24,4096]{1,0:T(8,128)S(1)} %collective-permute-done.4), channel_id=1, source_target_pairs={{0,16},{16,32},{32,48},{48,64},{64,80},{80,96},{96,112},{112,128},... | collective-permute-start | bytes 1179656 | tf_op jit(solution)/shard_map/ppermute | solution.py:15
  96.9 50.8 %collective-permute-start.1 = (f32[128,4096]{0,1:T(8,128)}, f32[128,4096]{0,1:T(8,128)}, u32[]{:S(2)}, u32[]{:S(2)}) collective-permute-start(f32[128,4096]{0,1:T(8,128)} %bitcast_add_fusion.2), channel_id=1, source_target_pairs={{0,1},{1,0},{2,3},{3,2},{4,5},{5,4},{6,7},{7,6},{8,9},{9,8},{10,11... | collective-permute-start | bytes 6291464 | tf_op jit(solution)/shard_map/ppermute | solution.py:73
  100.7 7.6 %collective-permute-start.12 = (f32[24,4096]{1,0:T(8,128)S(1)}, f32[24,4096]{1,0:T(8,128)}, u32[]{:S(2)}, u32[]{:S(2)}) collective-permute-start(f32[24,4096]{1,0:T(8,128)S(1)} %fusion.28), channel_id=1, source_target_pairs={{0,240},{16,0},{32,16},{48,32},{64,48},{80,64},{96,80},{112,96},{1... | collective-permute-start | bytes 1179656 | tf_op jit(solution)/shard_map/ppermute | solution.py:17
  102.1 8.0 %collective-permute-start.6 = (f32[24,4096]{1,0:T(8,128)S(1)}, f32[24,4096]{1,0:T(8,128)}, u32[]{:S(2)}, u32[]{:S(2)}) collective-permute-start(f32[24,4096]{1,0:T(8,128)S(1)} %collective-permute-done.5), channel_id=1, source_target_pairs={{0,16},{16,32},{32,48},{48,64},{64,80},{80,96},{96,112},{112,128},... | collective-permute-start | bytes 1179656 | tf_op jit(solution)/shard_map/ppermute | solution.py:15
  108.3 7.8 %collective-permute-start.13 = (f32[24,4096]{1,0:T(8,128)}, f32[24,4096]{1,0:T(8,128)}, u32[]{:S(2)}, u32[]{:S(2)}) collective-permute-start(f32[24,4096]{1,0:T(8,128)} %collective-permute-done.12), channel_id=1, source_target_pairs={{0,240},{16,0},{32,16},{48,32},{64,48},{80,64},{96,80},{112,96},{1... | collective-permute-start | bytes 1179656 | tf_op jit(solution)/shard_map/ppermute | solution.py:17
  110.1 8.8 %collective-permute-start.7 = (f32[24,4096]{1,0:T(8,128)}, f32[24,4096]{1,0:T(8,128)}, u32[]{:S(2)}, u32[]{:S(2)}) collective-permute-start(f32[24,4096]{1,0:T(8,128)} %collective-permute-done.6), channel_id=1, source_target_pairs={{0,16},{16,32},{32,48},{48,64},{64,80},{80,96},{96,112},{112,128},... | collective-permute-start | bytes 1179656 | tf_op jit(solution)/shard_map/ppermute | solution.py:15
  116.1 7.8 %collective-permute-start.14 = (f32[24,4096]{1,0:T(8,128)}, f32[24,4096]{1,0:T(8,128)}, u32[]{:S(2)}, u32[]{:S(2)}) collective-permute-start(f32[24,4096]{1,0:T(8,128)} %collective-permute-done.13), channel_id=1, source_target_pairs={{0,240},{16,0},{32,16},{48,32},{64,48},{80,64},{96,80},{112,96},{1... | collective-permute-start | bytes 1179656 | tf_op jit(solution)/shard_map/ppermute | solution.py:17
  118.9 8.7 %collective-permute-start.8 = (f32[24,4096]{1,0:T(8,128)}, f32[24,4096]{1,0:T(8,128)}, u32[]{:S(2)}, u32[]{:S(2)}) collective-permute-start(f32[24,4096]{1,0:T(8,128)} %collective-permute-done.7), channel_id=1, source_target_pairs={{0,16},{16,32},{32,48},{48,64},{64,80},{80,96},{96,112},{112,128},... | collective-permute-start | bytes 1179656 | tf_op jit(solution)/shard_map/ppermute | solution.py:15
  123.9 7.9 %collective-permute-start.15 = (f32[24,4096]{1,0:T(8,128)}, f32[24,4096]{1,0:T(8,128)}, u32[]{:S(2)}, u32[]{:S(2)}) collective-permute-start(f32[24,4096]{1,0:T(8,128)} %collective-permute-done.14), channel_id=1, source_target_pairs={{0,240},{16,0},{32,16},{48,32},{64,48},{80,64},{96,80},{112,96},{1... | collective-permute-start | bytes 1179656 | tf_op jit(solution)/shard_map/ppermute | solution.py:17
  127.6 8.7 %collective-permute-start.9 = (f32[24,4096]{1,0:T(8,128)}, f32[24,4096]{1,0:T(8,128)}, u32[]{:S(2)}, u32[]{:S(2)}) collective-permute-start(f32[24,4096]{1,0:T(8,128)} %collective-permute-done.8), channel_id=1, source_target_pairs={{0,16},{16,32},{32,48},{48,64},{64,80},{80,96},{96,112},{112,128},... | collective-permute-start | bytes 1179656 | tf_op jit(solution)/shard_map/ppermute | solution.py:15
  131.8 12.6 %collective-permute-start.16 = (f32[24,4096]{1,0:T(8,128)}, f32[24,4096]{1,0:T(8,128)}, u32[]{:S(2)}, u32[]{:S(2)}) collective-permute-start(f32[24,4096]{1,0:T(8,128)} %collective-permute-done.15), channel_id=1, source_target_pairs={{0,240},{16,0},{32,16},{48,32},{64,48},{80,64},{96,80},{112,96},{1... | collective-permute-start | bytes 1179656 | tf_op jit(solution)/shard_map/ppermute | solution.py:17
  136.4 11.3 %collective-permute-start.10 = (f32[24,4096]{1,0:T(8,128)}, f32[24,4096]{1,0:T(8,128)}, u32[]{:S(2)}, u32[]{:S(2)}) collective-permute-start(f32[24,4096]{1,0:T(8,128)} %collective-permute-done.9), channel_id=1, source_target_pairs={{0,16},{16,32},{32,48},{48,64},{64,80},{80,96},{96,112},{112,128},... | collective-permute-start | bytes 1179656 | tf_op jit(solution)/shard_map/ppermute | solution.py:15
  144.5 7.4 %collective-permute-start.17 = (f32[24,4096]{1,0:T(8,128)}, f32[24,4096]{1,0:T(8,128)S(1)}, u32[]{:S(2)}, u32[]{:S(2)}) collective-permute-start(f32[24,4096]{1,0:T(8,128)} %collective-permute-done.16), channel_id=1, source_target_pairs={{0,240},{16,0},{32,16},{48,32},{64,48},{80,64},{96,80},{112,96},{1... | collective-permute-start | bytes 1179656 | tf_op jit(solution)/shard_map/ppermute | solution.py:17
  147.6 8.6 %collective-permute-start.11 = (f32[24,4096]{1,0:T(8,128)}, f32[24,4096]{1,0:T(8,128)S(1)}, u32[]{:S(2)}, u32[]{:S(2)}) collective-permute-start(f32[24,4096]{1,0:T(8,128)} %collective-permute-done.10), channel_id=1, source_target_pairs={{0,16},{16,32},{32,48},{48,64},{64,80},{80,96},{96,112},{112,128},... | collective-permute-start | bytes 1179656 | tf_op jit(solution)/shard_map/ppermute | solution.py:15
  151.9 26.0 %collective-permute-start.18 = (f32[24,4096]{1,0:T(8,128)S(1)}, f32[24,4096]{1,0:T(8,128)S(1)}, u32[]{:S(2)}, u32[]{:S(2)}) collective-permute-start(f32[24,4096]{1,0:T(8,128)S(1)} %collective-permute-done.17), channel_id=1, source_target_pairs={{0,240},{16,0},{32,16},{48,32},{64,48},{80,64},{96,80},{112,96},{1... | collective-permute-start | bytes 1179656 | tf_op jit(solution)/shard_map/ppermute | solution.py:17
  171.7 29.5 %copy-start = (f32[1,128,4096]{1,2,0:T(8,128)S(1)}, f32[1,128,4096]{1,2,0:T(8,128)}, u32[]{:S(2)}) copy-start(f32[1,128,4096]{1,2,0:T(8,128)} %bitcast_add_fusion.4) | copy-start | bytes 6291460
  201.2 9.5 %copy-start.1 = (f32[1,128,4096]{1,2,0:T(8,128)S(1)}, f32[1,128,4096]{1,2,0:T(8,128)}, u32[]{:S(2)}) copy-start(f32[1,128,4096]{1,2,0:T(8,128)} %bitcast_add_fusion.5) | copy-start | bytes 6291460
  201.2 19.2 %copy-start.2 = (f32[128,4096]{0,1:T(8,128)S(1)}, f32[128,4096]{0,1:T(8,128)}, u32[]{:S(2)}) copy-start(f32[128,4096]{0,1:T(8,128)} %fusion.13) | copy-start | bytes 6291460
  227.6 7.3 %copy-start.9 = (s32[8,2]{0,1:T(2,128)S(1)}, s32[8,2]{0,1:T(2,128)}, u32[]{:S(2)}) copy-start(s32[8,2]{0,1:T(2,128)} %param.13) | copy-start | bytes 196
  227.6 7.3 %copy-start.8 = (f32[200]{0:T(256)S(1)}, f32[200]{0:T(256)}, u32[]{:S(2)}) copy-start(f32[200]{0:T(256)} %param.14) | copy-start | bytes 2404
  227.6 14.2 %copy-start.7 = (f32[384]{0:T(512)S(1)}, f32[384]{0:T(512)}, u32[]{:S(2)}) copy-start(f32[384]{0:T(512)} %param.15) | copy-start | bytes 4612
  227.6 14.2 %all-to-all-start = ((f32[16,8,384]{2,1,0:T(8,128)}), f32[16,8,384]{2,1,0:T(8,128)S(1)}, u32[]{:S(2)}, u32[]{:S(2)}) async-start(f32[16,8,384]{2,1,0:T(8,128)} %bitcast.42), calls=%async_computation | async-start | bytes 393216 | tf_op jit(solution)/shard_map/all_to_all | solution.py:97
  241.8 0.7 copy-start.4
Sparse Core Ops, SparseCore 0:
  9.8 79.7 all-gather.5
